TPU v7x, 512 devices: a whole 4x4x16 slice. The times are simulated.
512 devices in a mesh: space: 16 (over z), chaos: 32 (over x, y, core).
Axes of the slice: x: 4, y: 4, z: 16, core: 2. Of those that a mesh axis runs over, the one named last changes fastest.
Arguments:
- forcing: float32 [960, 64, 128], P('chaos', 'space'), may hold values from -120 to 120
- mean_field: float32 [64, 128], P('space'), may hold values from 1 to 8
- modes: float32 [12, 64, 128], P(None, 'space'), may hold values from 0.02 to 0.05
- lengths: int32 [32], replicated, may hold values from 1 to 30, 455 in all
Outputs:
- solution: float32 [960, 64, 128], P('chaos', 'space')
- norms: float32 [3], replicated
Inputs may be any that keep to these rules, and one draw needn't show every extreme that they name: Group lengths are positive, sum to 455, and the largest is exactly 30.
All inputs are finite; a program needn't handle non-finite values.
Results may differ from a plain program's by a relative error of at most 0.0001.
Values sent between devices are 32-bit elements; how exact they have to be, the bound alone decides.
No kernel may reach another device: no remote copies, remote signals or barrier semaphores. Data moves between devices by JAX's collectives and lax.ppermute only.
A program may use at most 64 MiB of HBM per device.

v0:
```python
import math

import jax
import jax.numpy as jnp
import numpy as np
from jax import lax
from jax.sharding import PartitionSpec as P

M = 12
P_SIZE = 455
ITERS = 3


spectrum_low = 0.05
spectrum_high = 3.0


def padded(shard, sides, width):
    for axis, dim in sides:
        devices, length = (lax.axis_size(axis), shard.shape[dim])
        up = [(i, (i + 1) % devices) for i in range(devices - 1)]
        down = [(j, i) for i, j in up]
        last = lax.slice_in_dim(shard, length - width, length, axis=dim)
        first = lax.slice_in_dim(shard, 0, width, axis=dim)
        before = lax.ppermute(last, axis, up)
        after = lax.ppermute(first, axis, down)
        shard = jnp.concatenate([before, shard, after], axis=dim)
    return shard


def index_key(entry):
    return tuple((int(value) for value in entry))


def chaos_tables(terms):
    indices = [np.zeros(terms, dtype=np.int64)]
    for first in range(terms):
        entry = np.zeros(terms, dtype=np.int64)
        entry[first] += 1
        indices.append(entry)
    for first in range(terms):
        for second in range(first, terms):
            entry = np.zeros(terms, dtype=np.int64)
            entry[first] += 1
            entry[second] += 1
            indices.append(entry)
    for first in range(terms):
        for second in range(first, terms):
            for third in range(second, terms):
                entry = np.zeros(terms, dtype=np.int64)
                entry[first] += 1
                entry[second] += 1
                entry[third] += 1
                indices.append(entry)
    lookup = {}
    for number, entry in enumerate(indices):
        lookup[index_key(entry)] = number
    count = len(indices)
    upward = np.full((count, terms), count, dtype=np.int64)
    downward = np.full((count, terms), count, dtype=np.int64)
    up_coef = np.zeros((count, terms))
    down_coef = np.zeros((count, terms))
    for number, entry in enumerate(indices):
        for term in range(terms):
            if entry.sum() < 3:
                other = entry.copy()
                other[term] += 1
                upward[number, term] = lookup[index_key(other)]
                up_coef[number, term] = math.sqrt(entry[term] + 1)
            if entry[term] > 0:
                other = entry.copy()
                other[term] -= 1
                downward[number, term] = lookup[index_key(other)]
                down_coef[number, term] = math.sqrt(entry[term])
    return (
        upward.astype(np.int32),
        downward.astype(np.int32),
        up_coef.astype(np.float32),
        down_coef.astype(np.float32),
    )


def shifted(values, toward):
    blank = jnp.zeros_like(values[..., :1])
    if toward > 0:
        return jnp.concatenate([values[..., 1:], blank], axis=-1)
    return jnp.concatenate([blank, values[..., :-1]], axis=-1)


def stiffness(field_pad, tile_pad):
    center_field = field_pad[..., 1:-1, :]
    center_tile = tile_pad[..., 1:-1, :]
    result = 0.5 * (center_field + field_pad[..., :-2, :]) * (center_tile - tile_pad[..., :-2, :])
    result = result + 0.5 * (center_field + field_pad[..., 2:, :]) * (
        center_tile - tile_pad[..., 2:, :]
    )
    for toward in (1, -1):
        result = result + 0.5 * (center_field + shifted(center_field, toward)) * (
            center_tile - shifted(center_tile, toward)
        )
    return result


def diagonal_of(field_pad):
    center_field = field_pad[..., 1:-1, :]
    result = 0.5 * (center_field + field_pad[..., :-2, :])
    result = result + 0.5 * (center_field + field_pad[..., 2:, :])
    for toward in (1, -1):
        result = result + 0.5 * (center_field + shifted(center_field, toward))
    return result


def local(forcing, mean_field, modes, lengths):
    slot_cap, tile_rows, tile_cols = forcing.shape
    groups = lax.axis_size("chaos")
    slot_count = slot_cap * groups
    my_group = lax.axis_index("chaos")
    upward, downward, up_coef, down_coef = chaos_tables(M)
    group_ends = jnp.cumsum(lengths).astype(jnp.int32)
    group_starts = (group_ends - lengths).astype(jnp.int32)
    slot_index = jnp.arange(slot_cap, dtype=jnp.int32)
    live_grid = slot_index[None, :] < lengths[:, None]
    ids_grid = jnp.where(live_grid, group_starts[:, None] + slot_index[None, :], -1).astype(
        jnp.int32
    )
    all_ids = ids_grid.reshape(slot_count)
    mine = lax.dynamic_slice_in_dim(ids_grid, my_group, 1, 0)[0]
    my_live = mine >= 0
    safe_ids = jnp.clip(mine, 0, P_SIZE - 1)
    up_rows = jnp.take(jnp.asarray(upward), safe_ids, axis=0)
    down_rows = jnp.take(jnp.asarray(downward), safe_ids, axis=0)
    live_float = my_live.astype(jnp.float32)
    up_weight = jnp.take(jnp.asarray(up_coef), safe_ids, axis=0) * live_float[:, None]
    down_weight = jnp.take(jnp.asarray(down_coef), safe_ids, axis=0) * live_float[:, None]
    coupling = jnp.where(
        up_rows.T[:, :, None] == all_ids[None, None, :], up_weight.T[:, :, None], 0.0
    )
    coupling = coupling + jnp.where(
        down_rows.T[:, :, None] == all_ids[None, None, :], down_weight.T[:, :, None], 0.0
    )
    coupling = coupling.reshape(M * slot_cap, slot_count)
    raw_fields = jnp.concatenate([mean_field[None], modes], axis=0)
    raw_pad = padded(raw_fields, (("space", 1),), 1)
    fields_pad = jnp.concatenate([raw_pad[:1], raw_pad[:1] * raw_pad[1:]], axis=0)
    diagonal = diagonal_of(raw_pad[0])
    theta = (spectrum_high + spectrum_low) / 2.0
    delta = (spectrum_high - spectrum_low) / 2.0
    sigma = theta / delta
    rho = 1.0 / sigma
    residual = forcing * live_float[:, None, None]
    solution = jnp.zeros_like(residual)
    direction = residual / diagonal / theta
    norm_list = []
    for sweep_index in range(ITERS):
        solution = solution + direction
        initial = jnp.zeros((M * slot_cap, tile_rows * tile_cols), jnp.float32)
        piece = jax.tree.map(
            lambda part: lax.all_gather(part, "chaos", axis=0, tiled=True), direction
        )
        count = piece.shape[0]
        block = lax.slice_in_dim(coupling, 0, count, axis=1)
        mixed = initial + jnp.dot(
            block,
            piece.reshape(count, -1),
            precision=lax.Precision.HIGHEST,
            preferred_element_type=jnp.float32,
        )
        mixed = mixed.reshape(M, slot_cap, tile_rows, tile_cols)
        stacked = jnp.concatenate([direction[None], mixed], axis=0)
        stacked = padded(stacked, (("space", 2),), 1)
        residual = residual - jnp.sum(stiffness(fields_pad[:, None], stacked), axis=0)
        partial_value = jnp.sum(residual * residual)
        norm_list.append(jnp.sqrt(lax.psum(partial_value, ("space", "chaos"))))
        if sweep_index + 1 < ITERS:
            rho_new = 1.0 / (2.0 * sigma - rho)
            direction = rho_new * rho * direction + 2.0 * rho_new / delta * (residual / diagonal)
            rho = rho_new
    norms = jnp.stack(norm_list)
    return (solution, norms)


def solution(mesh):
    in_specs = (P("chaos", "space", None), P("space", None), P(None, "space", None), P())
    out_specs = (P("chaos", "space", None), P())
    return jax.shard_map(local, mesh=mesh, in_specs=in_specs, out_specs=out_specs, check_vma=False)
```

profile of v0, /device:TPU:1, one launch (start us, length us, event | category | flops | bytes accessed | tf_op | source)
XLA Modules:
  0.0 371.4 jit_solution(11172319493625132148)
XLA Ops:
  7.2 0.0 all-gather.4.cloned.1.call-start
  7.2 0.8 pad_maximum_fusion.19
  8.0 4.4 %collective-permute-start = (f32[13,1,128]{2,1,0:T(1,128)S(1)}, f32[13,1,128]{2,1,0:T(1,128)S(1)}, u32[]{:S(2)}, u32[]{:S(2)}) collective-permute-start(f32[13,1,128]{2,1,0:T(1,128)S(1)} %get-tuple-element.41), channel_id=1, source_target_pairs={{0,32},{32,64},{64,96},{96,128},{128,160},{160,192},{192,224},{224... | collective-permute-start | bytes 19976 | tf_op jit(solution)/shard_map/ppermute | solution.py:25
  12.4 1.3 collective-permute-start.1
  13.7 0.8 fusion.94
  14.5 0.7 copy.30
  15.3 0.1 reduce-window.9
  15.3 0.1 reduce
  15.5 0.7 sub.48
  16.1 0.7 add_select_fusion
  16.9 0.1 collective-permute-done.1
  17.0 0.9 fusion.83
  17.8 0.9 fusion.91
  18.8 0.7 copy.36
  19.5 0.0 all-gather.6.cloned.1.call-start
  19.5 0.1 select_n.56
  19.6 1.5 gather_fusion.3
  21.2 1.5 gather_fusion.2
  22.7 1.5 gather_fusion.1
  24.2 0.1 fusion.77
  24.3 0.1 copy.33
  24.4 0.1 copy.35
  24.4 1.5 gather_fusion
  26.0 0.1 select_bitcast_fusion.1
  26.0 0.1 copy.32
  26.1 0.1 copy.34
  26.2 0.7 pad_maximum_fusion.20
  26.9 0.8 fusion.71
  27.7 0.1 fusion.93
  27.8 57.6 %all-gather.4.cloned.1.call-done = f32[960,4,128]{2,1,0:T(4,128)} async-done(((f32[30,4,128]{2,1,0:T(4,128)}), f32[960,4,128]{2,1,0:T(4,128)}) %all-gather.4.cloned.1.call-update) | async-done | bytes 1966096 | tf_op jit(solution)/shard_map/all_gather | solution.py:158
  85.3 4.5 %fusion.4 = f32[12,30,4,128]{3,1,2,0:T(8,128)S(1)} fusion(f32[12,30]{1,0:T(8,128)S(1)} %copy.35, s32[12,30]{1,0:T(8,128)S(1)} %copy.34, f32[12,30]{1,0:T(8,128)S(1)} %copy.33, s32[960]{0:T(1024)S(1)} %select_n.56, s32[12,30]{1,0:T(8,128)S(1)} %copy.32, f32[120,8,4,128]{3,2,1,0:T(4,128)} %bitcast.120), kind=kOutput, calls=%fused_computation.29 | convolution fusion | flops 2125094400 | bytes 2712960 | tf_op jit(solution)/shard_map/dot_general | solution.py:162
  89.9 3.2 collective-permute-start.2
  93.1 1.3 collective-permute-start.3
  94.4 0.1 fusion.75
  94.5 0.3 fusion.19
  94.8 2.6 collective-permute-done.2
  97.4 3.8 %collective-permute-done.3 = f32[13,30,1,128]{3,1,2,0:T(8,128)S(1)} collective-permute-done((f32[13,30,1,128]{3,1,2,0:T(8,128)S(1)}, f32[13,30,1,128]{3,1,2,0:T(8,128)S(1)}, u32[]{:S(2)}, u32[]{:S(2)}) %collective-permute-start.3) | collective-permute-done | bytes 199712 | tf_op jit(solution)/shard_map/ppermute | solution.py:26
  101.2 0.6 fusion.42
  101.8 0.2 copy-done
  102.0 0.1 multiply_add_fusion.1
  102.1 0.7 copy.38
  102.8 0.0 all-gather.8.cloned.1.call-start
  102.9 59.5 %all-gather.6.cloned.1.call-done = f32[960,4,128]{2,1,0:T(4,128)} async-done(((f32[30,4,128]{2,1,0:T(4,128)}), f32[960,4,128]{2,1,0:T(4,128)}) %all-gather.6.cloned.1.call-update) | async-done | bytes 1966096 | tf_op jit(solution)/shard_map/all_gather | solution.py:158
  162.4 4.5 %fusion.2 = f32[12,30,4,128]{3,1,2,0:T(8,128)S(1)} fusion(f32[12,30]{1,0:T(8,128)S(1)} %copy.35, s32[12,30]{1,0:T(8,128)S(1)} %copy.34, f32[12,30]{1,0:T(8,128)S(1)} %copy.33, s32[960]{0:T(1024)S(1)} %select_n.56, s32[12,30]{1,0:T(8,128)S(1)} %copy.32, f32[120,8,4,128]{3,2,1,0:T(4,128)} %bitcast.122), kind=kOutput, calls=%fused_computation.26 | convolution fusion | flops 2125094400 | bytes 2712960 | tf_op jit(solution)/shard_map/dot_general | solution.py:162
  167.0 3.2 collective-permute-start.4
  170.2 1.3 collective-permute-start.5
  171.5 0.3 fusion.17
  171.8 2.7 collective-permute-done.4
  174.4 3.8 %collective-permute-done.5 = f32[13,30,1,128]{3,1,2,0:T(8,128)S(1)} collective-permute-done((f32[13,30,1,128]{3,1,2,0:T(8,128)S(1)}, f32[13,30,1,128]{3,1,2,0:T(8,128)S(1)}, u32[]{:S(2)}, u32[]{:S(2)}) %collective-permute-start.5) | collective-permute-done | bytes 199712 | tf_op jit(solution)/shard_map/ppermute | solution.py:26
  178.3 0.6 fusion.34
  178.9 0.7 add_add_fusion
  179.6 0.7 copy.40
  180.3 59.6 %all-gather.8.cloned.1.call-done = f32[960,4,128]{2,1,0:T(4,128)} async-done(((f32[30,4,128]{2,1,0:T(4,128)}), f32[960,4,128]{2,1,0:T(4,128)}) %all-gather.8.cloned.1.call-update) | async-done | bytes 1966096 | tf_op jit(solution)/shard_map/all_gather | solution.py:158
  239.9 4.5 %fusion = f32[12,30,4,128]{3,1,2,0:T(8,128)S(1)} fusion(f32[12,30]{1,0:T(8,128)S(1)} %copy.35, s32[12,30]{1,0:T(8,128)S(1)} %copy.34, f32[12,30]{1,0:T(8,128)S(1)} %copy.33, s32[960]{0:T(1024)S(1)} %select_n.56, s32[12,30]{1,0:T(8,128)S(1)} %copy.32, f32[120,8,4,128]{3,2,1,0:T(4,128)} %bitcast.121), kind=kOutput, calls=%fused_computation.23 | convolution fusion | flops 2125094400 | bytes 2712960 | tf_op jit(solution)/shard_map/dot_general | solution.py:162
  244.4 3.2 collective-permute-start.6
  247.6 1.3 collective-permute-start.7
  248.9 0.7 copy.42
  249.6 0.3 fusion.15
  249.9 2.0 collective-permute-done.6
  251.9 3.8 %collective-permute-done.7 = f32[13,30,1,128]{3,1,2,0:T(8,128)S(1)} collective-permute-done((f32[13,30,1,128]{3,1,2,0:T(8,128)S(1)}, f32[13,30,1,128]{3,1,2,0:T(8,128)S(1)}, u32[]{:S(2)}, u32[]{:S(2)}) %collective-permute-start.7) | collective-permute-done | bytes 199712 | tf_op jit(solution)/shard_map/ppermute | solution.py:26
  255.8 0.6 fusion.26
  256.4 0.7 multiply_reduce_fusion.1
  257.1 105.2 %all-reduce.10 = (f32[]{:T(128)}, f32[]{:T(128)}, f32[]{:T(128)}) all-reduce(f32[]{:T(128)} %get-tuple-element.11, f32[]{:T(128)} %get-tuple-element.10, f32[]{:T(128)} %get-tuple-element.32), channel_id=1, replica_groups=mesh['space'=16,'chaos'=32] {'space','chaos'}, use_global_device_ids=true, to_apply=%region_9.12 | all-reduce | flops 3 | bytes 24 | tf_op jit(solution)/shard_map/psum | solution.py:173
  364.3 0.6 pad_maximum_fusion.25
  (12 shorter events, 0.2 us)
Async XLA Ops:
  7.2 78.2 %all-gather.4.cloned.1.call-start = ((), (), s32[]{:S(2)}) async-start(), calls=%async_computation | async-start | bytes 2027520 | tf_op jit(solution)/shard_map/all_gather | solution.py:158
  8.0 8.8 %collective-permute-start = (f32[13,1,128]{2,1,0:T(1,128)S(1)}, f32[13,1,128]{2,1,0:T(1,128)S(1)}, u32[]{:S(2)}, u32[]{:S(2)}) collective-permute-start(f32[13,1,128]{2,1,0:T(1,128)S(1)} %get-tuple-element.41), channel_id=1, source_target_pairs={{0,32},{32,64},{64,96},{96,128},{128,160},{160,192},{192,224},{224... | collective-permute-start | bytes 19976 | tf_op jit(solution)/shard_map/ppermute | solution.py:25
  12.4 4.6 %collective-permute-start.1 = (f32[13,1,128]{2,1,0:T(1,128)S(1)}, f32[13,1,128]{2,1,0:T(1,128)S(1)}, u32[]{:S(2)}, u32[]{:S(2)}) collective-permute-start(f32[13,1,128]{2,1,0:T(1,128)S(1)} %get-tuple-element.42), channel_id=1, source_target_pairs={{32,0},{64,32},{96,64},{128,96},{160,128},{192,160},{224,192},{256... | collective-permute-start | bytes 19976 | tf_op jit(solution)/shard_map/ppermute | solution.py:26
  19.5 143.0 %all-gather.6.cloned.1.call-start = ((), (), s32[]{:S(2)}) async-start(), calls=%async_computation.1 | async-start | bytes 2027520 | tf_op jit(solution)/shard_map/all_gather | solution.py:158
  89.9 7.5 %collective-permute-start.2 = (f32[13,30,1,128]{3,1,2,0:T(8,128)S(1)}, f32[13,30,1,128]{3,1,2,0:T(8,128)S(1)}, u32[]{:S(2)}, u32[]{:S(2)}) collective-permute-start(f32[13,30,1,128]{3,1,2,0:T(8,128)S(1)} %get-tuple-element.30), channel_id=1, source_target_pairs={{0,32},{32,64},{64,96},{96,128},{128,160},{160,192},{192,224},{224... | collective-permute-start | bytes 599048 | tf_op jit(solution)/shard_map/ppermute | solution.py:25
  93.1 8.1 %collective-permute-start.3 = (f32[13,30,1,128]{3,1,2,0:T(8,128)S(1)}, f32[13,30,1,128]{3,1,2,0:T(8,128)S(1)}, u32[]{:S(2)}, u32[]{:S(2)}) collective-permute-start(f32[13,30,1,128]{3,1,2,0:T(8,128)S(1)} %get-tuple-element.31), channel_id=1, source_target_pairs={{32,0},{64,32},{96,64},{128,96},{160,128},{192,160},{224,192},{256... | collective-permute-start | bytes 599048 | tf_op jit(solution)/shard_map/ppermute | solution.py:26
  101.2 0.8 copy-start
  102.8 137.1 %all-gather.8.cloned.1.call-start = ((), (), s32[]{:S(2)}) async-start(), calls=%async_computation.2 | async-start | bytes 2027520 | tf_op jit(solution)/shard_map/all_gather | solution.py:158
  167.0 7.5 %collective-permute-start.4 = (f32[13,30,1,128]{3,1,2,0:T(8,128)S(1)}, f32[13,30,1,128]{3,1,2,0:T(8,128)S(1)}, u32[]{:S(2)}, u32[]{:S(2)}) collective-permute-start(f32[13,30,1,128]{3,1,2,0:T(8,128)S(1)} %get-tuple-element.26), channel_id=1, source_target_pairs={{0,32},{32,64},{64,96},{96,128},{128,160},{160,192},{192,224},{224... | collective-permute-start | bytes 599048 | tf_op jit(solution)/shard_map/ppermute | solution.py:25
  170.2 8.1 %collective-permute-start.5 = (f32[13,30,1,128]{3,1,2,0:T(8,128)S(1)}, f32[13,30,1,128]{3,1,2,0:T(8,128)S(1)}, u32[]{:S(2)}, u32[]{:S(2)}) collective-permute-start(f32[13,30,1,128]{3,1,2,0:T(8,128)S(1)} %get-tuple-element.27), channel_id=1, source_target_pairs={{32,0},{64,32},{96,64},{128,96},{160,128},{192,160},{224,192},{256... | collective-permute-start | bytes 599048 | tf_op jit(solution)/shard_map/ppermute | solution.py:26
  244.4 7.5 %collective-permute-start.6 = (f32[13,30,1,128]{3,1,2,0:T(8,128)S(1)}, f32[13,30,1,128]{3,1,2,0:T(8,128)S(1)}, u32[]{:S(2)}, u32[]{:S(2)}) collective-permute-start(f32[13,30,1,128]{3,1,2,0:T(8,128)S(1)} %get-tuple-element.22), channel_id=1, source_target_pairs={{0,32},{32,64},{64,96},{96,128},{128,160},{160,192},{192,224},{224... | collective-permute-start | bytes 599048 | tf_op jit(solution)/shard_map/ppermute | solution.py:25
  247.6 8.1 %collective-permute-start.7 = (f32[13,30,1,128]{3,1,2,0:T(8,128)S(1)}, f32[13,30,1,128]{3,1,2,0:T(8,128)S(1)}, u32[]{:S(2)}, u32[]{:S(2)}) collective-permute-start(f32[13,30,1,128]{3,1,2,0:T(8,128)S(1)} %get-tuple-element.23), channel_id=1, source_target_pairs={{32,0},{64,32},{96,64},{128,96},{160,128},{192,160},{224,192},{256... | collective-permute-start | bytes 599048 | tf_op jit(solution)/shard_map/ppermute | solution.py:26
Sparse Core Ops, SparseCore 0:
  19.6 65.7 all-gather.3
  102.9 59.4 all-gather.5
  180.4 59.4 all-gather.7
where the time goes:
time: 372 us; the launch traced here: 371 us
  waiting for transfers between devices  196 us (53%)
  blocking collectives  105 us (28%)
  starting transfers between devices  19.2 us (5%)
  between operations  16 us (4%)
  matrix products  13.5 us (4%)
  local copies, waits for them, and re-layouts  11 us (3%)
  other arithmetic  10.8 us (3%)
    all_gather x3, waiting for transfers between devices, local(): lax.all_gather(part, 'chaos', axis=0, tiled=True)  177 us
    psum x1, blocking collectives, local(): norm_list.append(jnp.sqrt(lax.psum(partial_value, ('space', 'chaos'))))  105 us
    ppermute x4, starting transfers between devices, padded(): before = lax.ppermute(last, axis, up)  13.9 us
    dot_general x3, matrix products, local(): jnp.dot(block, piece.reshape(count, -1), precision=lax.Precision.HIGHEST,...  13.5 us
    ppermute x4, waiting for transfers between devices, padded(): after = lax.ppermute(first, axis, down)  11.6 us
  transfers between devices with their start and end apart: 11, of which 10 were waited for; matrix products, arithmetic and copies ran while one was open for 4% of the time, Pallas kernels for 0%

commit v1 on v0

v1 whole, which is shorter than its diff:
```python
import math

import jax
import jax.numpy as jnp
import numpy as np
from jax import lax
from jax.sharding import PartitionSpec as P

M = 12
P_SIZE = 455
ITERS = 3
GHOST = ITERS + 1


spectrum_low = 0.05
spectrum_high = 3.0


def index_key(entry):
    return tuple((int(value) for value in entry))


def chaos_tables(terms):
    indices = [np.zeros(terms, dtype=np.int64)]
    for first in range(terms):
        entry = np.zeros(terms, dtype=np.int64)
        entry[first] += 1
        indices.append(entry)
    for first in range(terms):
        for second in range(first, terms):
            entry = np.zeros(terms, dtype=np.int64)
            entry[first] += 1
            entry[second] += 1
            indices.append(entry)
    for first in range(terms):
        for second in range(first, terms):
            for third in range(second, terms):
                entry = np.zeros(terms, dtype=np.int64)
                entry[first] += 1
                entry[second] += 1
                entry[third] += 1
                indices.append(entry)
    lookup = {}
    for number, entry in enumerate(indices):
        lookup[index_key(entry)] = number
    count = len(indices)
    upward = np.full((count, terms), count, dtype=np.int64)
    downward = np.full((count, terms), count, dtype=np.int64)
    up_coef = np.zeros((count, terms))
    down_coef = np.zeros((count, terms))
    for number, entry in enumerate(indices):
        for term in range(terms):
            if entry.sum() < 3:
                other = entry.copy()
                other[term] += 1
                upward[number, term] = lookup[index_key(other)]
                up_coef[number, term] = math.sqrt(entry[term] + 1)
            if entry[term] > 0:
                other = entry.copy()
                other[term] -= 1
                downward[number, term] = lookup[index_key(other)]
                down_coef[number, term] = math.sqrt(entry[term])
    return (
        upward.astype(np.int32),
        downward.astype(np.int32),
        up_coef.astype(np.float32),
        down_coef.astype(np.float32),
    )


def neighbour(values, step):
    blank = jnp.zeros(values.shape[:-1] + (abs(step),), values.dtype)
    if step > 0:
        return jnp.concatenate([values[..., step:], blank], axis=-1)
    return jnp.concatenate([blank, values[..., :step]], axis=-1)


def local(forcing, mean_field, modes, lengths):
    cap, rows, cols = forcing.shape
    n_space = lax.axis_size("space")
    n_chaos = lax.axis_size("chaos")
    my_row_block = lax.axis_index("space")
    my_col_block = lax.axis_index("chaos")
    width = cols // n_chaos
    ghost = GHOST
    assert rows >= ghost and ghost % width == 0 and width * n_chaos == cols
    patch_rows, patch_cols = rows + 2 * ghost, width + 2 * ghost
    cells = patch_rows * patch_cols
    count = P_SIZE

    fields = jnp.concatenate([mean_field[None], mean_field[None] * modes], axis=0)
    block = jnp.concatenate([forcing, fields], axis=0)
    down_pairs = [(i, i + 1) for i in range(n_space - 1)]
    up_pairs = [(i + 1, i) for i in range(n_space - 1)]
    above = lax.ppermute(block[:, rows - ghost :], "space", down_pairs)
    below = lax.ppermute(block[:, :ghost], "space", up_pairs)
    tall = jnp.concatenate([above, block, below], axis=1)
    tall = jnp.pad(tall, ((0, 0), (0, 0), (ghost, ghost)))

    side = ghost // width
    pieces = tall.reshape(tall.shape[0], patch_rows, n_chaos + 2 * side, width)
    windows = jnp.concatenate(
        [pieces[:, :, j : j + n_chaos] for j in range(2 * side + 1)], axis=-1
    )
    sent = jnp.transpose(windows[:cap], (2, 0, 1, 3))
    got = lax.all_to_all(sent, "chaos", 0, 0, tiled=True)
    by_slot = got.reshape(n_chaos * cap, cells)
    my_fields = lax.dynamic_index_in_dim(windows[cap:], my_col_block, axis=2, keepdims=False)
    my_fields = my_fields.reshape(M + 1, cells)

    group_ends = jnp.cumsum(lengths).astype(jnp.int32)
    group_starts = (group_ends - lengths).astype(jnp.int32)
    coeff_index = jnp.arange(count, dtype=jnp.int32)
    owner = jnp.sum((coeff_index[:, None] >= group_ends[None, :]).astype(jnp.int32), axis=1)
    slot_of = (owner * cap + coeff_index - group_starts[owner]).astype(jnp.int32)
    rhs = jnp.take(by_slot, slot_of, axis=0)

    row_at = my_row_block * rows - ghost + jnp.arange(patch_rows)
    col_at = my_col_block * width - ghost + jnp.arange(patch_cols)
    inside = ((row_at >= 0) & (row_at < rows * n_space))[:, None] & (
        (col_at >= 0) & (col_at < cols)
    )[None, :]
    inside = inside.reshape(cells)
    local_rows = jnp.arange(patch_rows)
    local_cols = jnp.arange(patch_cols)
    own = ((local_rows >= ghost) & (local_rows < ghost + rows))[:, None] & (
        (local_cols >= ghost) & (local_cols < ghost + width)
    )[None, :]
    own = own.reshape(cells)

    steps = (-patch_cols, patch_cols, 1, -1)
    weights = jnp.stack([0.5 * (my_fields + neighbour(my_fields, s)) for s in steps], axis=1)
    mean_now = my_fields[0]
    diagonal = 0.5 * (mean_now + neighbour(mean_now, steps[0]))
    for s in steps[1:]:
        diagonal = diagonal + 0.5 * (mean_now + neighbour(mean_now, s))

    upward, downward, up_coef, down_coef = chaos_tables(M)
    rows_per_term = count + 1
    up_flat = (upward.T + rows_per_term * np.arange(M)[:, None]).reshape(-1)
    down_flat = (downward.T + rows_per_term * np.arange(M)[:, None]).reshape(-1)
    up_w = jnp.asarray(up_coef.T[:, :, None])
    down_w = jnp.asarray(down_coef.T[:, :, None])

    def operator(tiles):
        diffs = [tiles - neighbour(tiles, s) for s in steps]
        terms = weights[:, 0][:, None] * diffs[0][None]
        for n in range(1, 4):
            terms = terms + weights[:, n][:, None] * diffs[n][None]
        coupled = jnp.concatenate(
            [terms[1:], jnp.zeros((M, 1, cells), jnp.float32)], axis=1
        ).reshape(M * rows_per_term, cells)
        up_part = jnp.take(coupled, up_flat, axis=0).reshape(M, count, cells)
        down_part = jnp.take(coupled, down_flat, axis=0).reshape(M, count, cells)
        return terms[0] + jnp.sum(up_w * up_part + down_w * down_part, axis=0)

    theta = (spectrum_high + spectrum_low) / 2.0
    delta = (spectrum_high - spectrum_low) / 2.0
    sigma = theta / delta
    rho = 1.0 / sigma
    residual = rhs
    solution = jnp.zeros_like(rhs)
    direction = jnp.where(inside, residual / diagonal / theta, 0.0)
    partial_list = []
    for sweep_index in range(ITERS):
        solution = solution + direction
        residual = residual - operator(direction)
        partial_list.append(jnp.sum(jnp.where(own, residual * residual, 0.0)))
        if sweep_index + 1 < ITERS:
            rho_new = 1.0 / (2.0 * sigma - rho)
            direction = rho_new * rho * direction + 2.0 * rho_new / delta * (residual / diagonal)
            direction = jnp.where(inside, direction, 0.0)
            rho = rho_new
    partials = jnp.stack(partial_list)

    mine = solution.reshape(count, patch_rows, patch_cols)[
        :, ghost : ghost + rows, ghost : ghost + width
    ]
    mine = jnp.concatenate([mine, jnp.zeros((1, rows, width), jnp.float32)], axis=0)
    slot_index = jnp.arange(cap, dtype=jnp.int32)
    live = slot_index[None, :] < lengths[:, None]
    coeff_of_slot = jnp.where(live, group_starts[:, None] + slot_index[None, :], count)
    by_slot_out = jnp.take(mine, coeff_of_slot.reshape(-1), axis=0)
    chunk = cap * rows * width
    payload = jnp.concatenate(
        [
            by_slot_out.reshape(n_chaos, chunk),
            jnp.broadcast_to(partials[None, :], (n_chaos, ITERS)),
        ],
        axis=1,
    )
    back = lax.all_to_all(payload, "chaos", 0, 0, tiled=True)
    out = back[:, :chunk].reshape(n_chaos, cap, rows, width)
    out = jnp.transpose(out, (1, 2, 0, 3)).reshape(cap, rows, cols)
    row_sum = jnp.sum(back[:, chunk:], axis=0)
    norms = jnp.sqrt(lax.psum(row_sum, "space"))
    return (out, norms)


def solution(mesh):
    in_specs = (P("chaos", "space", None), P("space", None), P(None, "space", None), P())
    out_specs = (P("chaos", "space", None), P())
    return jax.shard_map(local, mesh=mesh, in_specs=in_specs, out_specs=out_specs, check_vma=False)
```

time: 372 us -> 387 us (1.040)
  the two profiles are of different devices: /device:TPU:1 before, /device:TPU:2 now
where the time goes in v1:
time: 387 us; the launch traced here: 381 us
  local copies, waits for them, and re-layouts  233 us (60%)
  other arithmetic  76.5 us (20%)
  blocking collectives  48.9 us (13%)
  starting transfers between devices  13 us (3%)
  waiting for transfers between devices  7.28 us (2%)
    gather x6, local copies, waits for them, and re-layouts, operator(): up_part = jnp.take(coupled, up_flat, axis=0).reshape(M, count, cells)  64.6 us
    gather x6, local copies, waits for them, and re-layouts, operator(): down_part = jnp.take(coupled, down_flat, axis=0).reshape(M, count, cells)  64.5 us
    psum x1, blocking collectives, local(): norms = jnp.sqrt(lax.psum(row_sum, 'space'))  37.2 us
    unnamed x58, local copies, waits for them, and re-layouts  19.1 us
    reduce_sum x3, other arithmetic, operator(): return terms[0] + jnp.sum(up_w * up_part + down_w * down_part, axis=0)  16.8 us
    reshape x3, local copies, waits for them, and re-layouts, operator(): down_part = jnp.take(coupled, down_flat, axis=0).reshape(M, count, cells)  16.1 us
    reshape x3, local copies, waits for them, and re-layouts, operator(): up_part = jnp.take(coupled, up_flat, axis=0).reshape(M, count, cells)  15.9 us
    and x1, other arithmetic, local(): rhs = jnp.take(by_slot, slot_of, axis=0)  15.7 us
  transfers between devices with their start and end apart: 3, of which 1 were waited for; matrix products, arithmetic and copies ran while one was open for 8% of the time, Pallas kernels for 0%

profile of v1, /device:TPU:2, one launch (start us, length us, event | category | flops | bytes accessed | tf_op | source)
XLA Modules:
  0.0 380.6 jit_solution(3179117209295791131)
XLA Ops:
  2.9 3.8 %collective-permute-start = (f32[43,4,128]{2,1,0:T(4,128)S(1)}, f32[43,4,128]{2,1,0:T(4,128)S(1)}, u32[]{:S(2)}, u32[]{:S(2)}) collective-permute-start(f32[43,4,128]{2,1,0:T(4,128)S(1)} %pad_maximum_fusion.2), channel_id=1, source_target_pairs={{0,32},{32,64},{64,96},{96,128},{128,160},{160,192},{192,224},{224... | collective-permute-start | bytes 264200 | tf_op jit(solution)/shard_map/ppermute | solution.py:95
  6.8 1.3 collective-permute-start.1
  13.5 4.3 %compare_select_fusion.4 = (s32[455,1]{0,1:T(1,128)S(1)}, s32[455,1]{0,1:T(1,128)S(1)}) fusion(s32[]{:T(128)} %bitcast.27, s32[]{:T(128)} %bitcast.28, s32[]{:T(128)} %bitcast.29, s32[]{:T(128)} %bitcast.30, s32[]{:T(128)} %bitcast.31, s32[]{:T(128)} %bitcast.33, s32[]{:T(128)} %bitcast.32, s32[455,1]{0,1:T(1,128)S(1)} %bitcast.120), kind=kLoop, calls=%fused_computation.100 | loop fusion | flops 6825 | bytes 5488 | tf_op jit(solution)/shard_map/gather | solution.py:115
  17.9 15.7 %compare_and_fusion.2 = (pred[455]{0:T(512)(128)(4,1)S(1)}, s32[455]{0:T(512)S(1)}) fusion(s32[455]{0:T(512)S(1)} %convert_reduce_fusion, pred[455]{0:T(512)(128)(4,1)S(1)} %get-tuple-element.39, pred[455]{0:T(512)(128)(4,1)S(1)} %get-tuple-element.38, pred[455]{0:T(512)(128)(4,1)S(1)} %get-tuple-element.37, pred[455]{0:T(512)(128)(4,1)S(1)} %get-tuple-element.36, ...), kind=kLoop, calls=%fused_computation.117 | loop fusion | flops 15470 | bytes 17390 | tf_op jit(solution)/shard_map/jit(_take)/and | solution.py:116
  40.7 1.5 copy-done.10
  42.3 2.9 reshape.541
  45.2 7.9 %all-to-all-start = ((f32[32,1,4320]{2,1,0:T(1,128)}), f32[32,1,4320]{2,1,0:T(1,128)S(1)}, u32[]{:S(2)}, u32[]{:S(2)}) async-start(f32[32,1,4320]{2,1,0:T(1,128)} %reshape.541), calls=%async_computation | async-start | bytes 1114112 | tf_op jit(solution)/shard_map/all_to_all | solution.py:106
  53.3 1.1 dynamic-slice_reduce_fusion.2
  55.8 7.3 %all-to-all-done = f32[32,1,4320]{2,1,0:T(1,128)S(1)} async-done(((f32[32,1,4320]{2,1,0:T(1,128)}), f32[32,1,4320]{2,1,0:T(1,128)S(1)}, u32[]{:S(2)}, u32[]{:S(2)}) %all-to-all-start) | async-done | bytes 552992 | tf_op jit(solution)/shard_map/all_to_all | solution.py:106
  63.5 2.8 reduce.57
  66.4 2.7 reshape.542
  69.2 2.8 copy.88
  71.9 3.0 reshape.302
  75.2 1.7 gather_fusion
  77.9 1.5 multiply_add_fusion.2
  79.8 2.2 copy-done
  82.0 2.9 concatenate.99
  84.9 16.7 %gather_fusion.2 = f32[5460,144]{1,0:T(8,128)} fusion(f32[5472,144]{1,0:T(8,128)} %bitcast.106, s32[6144]{0:T(1024)S(1)} %pad_clamp_fusion.1), kind=kCustom, calls=%fused_computation.clone | custom fusion | bytes 6311760 | tf_op jit(solution)/shard_map/jit(_take)/gather | solution.py:153
  101.6 4.3 %copy.94 = f32[5460,144]{0,1:T(8,128)S(1)} copy(f32[5460,144]{1,0:T(8,128)} %gather_fusion.2) | data formatting | bytes 6289920 | tf_op jit(solution)/shard_map/jit(_take)/gather | solution.py:153
  105.9 4.9 %reshape.305 = f32[12,455,144]{1,0,2:T(8,128)} reshape(f32[5460,144]{0,1:T(8,128)S(1)} %copy.94) | data formatting | bytes 6289920 | tf_op jit(solution)/shard_map/reshape | solution.py:153
  110.8 16.7 %gather_fusion.3 = f32[5460,144]{1,0:T(8,128)} fusion(f32[5472,144]{1,0:T(8,128)} %bitcast.107, s32[6144]{0:T(1024)S(1)} %pad_clamp_fusion), kind=kCustom, calls=%fused_computation.1.clone | custom fusion | bytes 6311760 | tf_op jit(solution)/shard_map/jit(_take)/gather | solution.py:154
  127.5 4.3 %copy.95 = f32[5460,144]{0,1:T(8,128)S(1)} copy(f32[5460,144]{1,0:T(8,128)} %gather_fusion.3) | data formatting | bytes 6289920 | tf_op jit(solution)/shard_map/jit(_take)/gather | solution.py:154
  131.8 4.7 %reshape.306 = f32[12,455,144]{1,0,2:T(8,128)} reshape(f32[5460,144]{0,1:T(8,128)S(1)} %copy.95) | data formatting | bytes 6289920 | tf_op jit(solution)/shard_map/reshape | solution.py:154
  136.5 5.6 %add_reduce_fusion.2 = f32[455,144]{0,1:T(8,128)S(1)} fusion(f32[12,455,144]{1,0,2:T(8,128)} %reshape.306, f32[12,455,144]{1,0,2:T(8,128)} %reshape.305, f32[12,455]{1,0:T(8,128)S(1)} %copy-done.16, f32[12,455]{1,0:T(8,128)S(1)} %copy-done.15), kind=kLoop, calls=%fused_computation.13 | loop fusion | flops 3079440 | bytes 6595680 | tf_op jit(solution)/shard_map/reduce_sum | solution.py:155
  142.3 1.3 add_select_fusion.1
  144.3 1.5 multiply_add_fusion.1
  146.2 2.2 copy-done.1
  148.4 2.9 concatenate.104
  151.3 16.8 %gather_fusion.4 = f32[5460,144]{1,0:T(8,128)} fusion(f32[5472,144]{1,0:T(8,128)} %bitcast.110, s32[6144]{0:T(1024)S(1)} %pad_clamp_fusion.1), kind=kCustom, calls=%fused_computation.2.clone | custom fusion | bytes 6311760 | tf_op jit(solution)/shard_map/jit(_take)/gather | solution.py:153
  168.1 16.7 %gather_fusion.5 = f32[5460,144]{1,0:T(8,128)} fusion(f32[5472,144]{1,0:T(8,128)} %bitcast.111, s32[6144]{0:T(1024)S(1)} %pad_clamp_fusion), kind=kCustom, calls=%fused_computation.3.clone | custom fusion | bytes 6311760 | tf_op jit(solution)/shard_map/jit(_take)/gather | solution.py:154
  184.8 5.9 %copy.100 = f32[5460,144]{0,1:T(8,128)} copy(f32[5460,144]{1,0:T(8,128)} %gather_fusion.4) | data formatting | bytes 6289920 | tf_op jit(solution)/shard_map/jit(_take)/gather | solution.py:153
  190.7 6.2 %reshape.308 = f32[12,455,144]{1,0,2:T(8,128)} reshape(f32[5460,144]{0,1:T(8,128)} %copy.100) | data formatting | bytes 6289920 | tf_op jit(solution)/shard_map/reshape | solution.py:153
  196.9 5.8 %copy.101 = f32[5460,144]{0,1:T(8,128)} copy(f32[5460,144]{1,0:T(8,128)} %gather_fusion.5) | data formatting | bytes 6289920 | tf_op jit(solution)/shard_map/jit(_take)/gather | solution.py:154
  202.8 6.6 %reshape.309 = f32[12,455,144]{1,0,2:T(8,128)} reshape(f32[5460,144]{0,1:T(8,128)} %copy.101) | data formatting | bytes 6289920 | tf_op jit(solution)/shard_map/reshape | solution.py:154
  209.4 5.6 %add_reduce_fusion.1 = f32[455,144]{0,1:T(8,128)S(1)} fusion(f32[12,455,144]{1,0,2:T(8,128)} %reshape.309, f32[12,455,144]{1,0,2:T(8,128)} %reshape.308, f32[12,455]{1,0:T(8,128)S(1)} %copy-done.16, f32[12,455]{1,0:T(8,128)S(1)} %copy-done.15), kind=kLoop, calls=%fused_computation.12 | loop fusion | flops 3079440 | bytes 6595680 | tf_op jit(solution)/shard_map/reduce_sum | solution.py:155
  215.2 2.0 add_select_fusion
  217.9 1.5 multiply_add_fusion
  219.8 2.2 copy-done.2
  222.0 2.9 concatenate.110
  224.9 16.7 %gather_fusion.6 = f32[5460,144]{1,0:T(8,128)} fusion(f32[5472,144]{1,0:T(8,128)} %bitcast.108, s32[6144]{0:T(1024)S(1)} %pad_clamp_fusion.1), kind=kCustom, calls=%fused_computation.4.clone | custom fusion | bytes 6311760 | tf_op jit(solution)/shard_map/jit(_take)/gather | solution.py:153
  241.6 16.8 %gather_fusion.7 = f32[5460,144]{1,0:T(8,128)} fusion(f32[5472,144]{1,0:T(8,128)} %bitcast.109, s32[6144]{0:T(1024)S(1)} %pad_clamp_fusion), kind=kCustom, calls=%fused_computation.5.clone | custom fusion | bytes 6311760 | tf_op jit(solution)/shard_map/jit(_take)/gather | solution.py:154
  260.0 3.6 reshape.507
  263.6 4.3 %copy.105 = f32[5460,144]{0,1:T(8,128)S(1)} copy(f32[5460,144]{1,0:T(8,128)} %gather_fusion.6) | data formatting | bytes 6289920 | tf_op jit(solution)/shard_map/jit(_take)/gather | solution.py:153
  267.8 4.7 %reshape.311 = f32[12,455,144]{1,0,2:T(8,128)} reshape(f32[5460,144]{0,1:T(8,128)S(1)} %copy.105) | data formatting | bytes 6289920 | tf_op jit(solution)/shard_map/reshape | solution.py:153
  272.5 4.3 %copy.106 = f32[5460,144]{0,1:T(8,128)S(1)} copy(f32[5460,144]{1,0:T(8,128)} %gather_fusion.7) | data formatting | bytes 6289920 | tf_op jit(solution)/shard_map/jit(_take)/gather | solution.py:154
  276.8 4.8 %reshape.312 = f32[12,455,144]{1,0,2:T(8,128)} reshape(f32[5460,144]{0,1:T(8,128)S(1)} %copy.106) | data formatting | bytes 6289920 | tf_op jit(solution)/shard_map/reshape | solution.py:154
  281.7 5.6 %add_reduce_fusion = f32[455,144]{0,1:T(8,128)S(1)} fusion(f32[12,455,144]{1,0,2:T(8,128)} %reshape.312, f32[12,455,144]{1,0,2:T(8,128)} %reshape.311, f32[12,455]{1,0:T(8,128)S(1)} %copy-done.16, f32[12,455]{1,0:T(8,128)S(1)} %copy-done.15), kind=kLoop, calls=%fused_computation.11 | loop fusion | flops 3079440 | bytes 6595680 | tf_op jit(solution)/shard_map/reduce_sum | solution.py:155
  287.3 1.0 copy.107
  288.3 2.7 copy.103
  291.1 3.5 reshape.510
  294.6 2.7 copy.97
  297.4 3.5 reshape.509
  300.8 3.8 %add.320 = f32[455,12,12]{2,1,0:T(8,128)S(1)} add(f32[455,12,12]{2,1,0:T(8,128)} %reshape.510, f32[455,12,12]{2,1,0:T(8,128)} %copy.103) | non-fusion elementwise | flops 65520 | bytes 786240 | tf_op jit(solution)/shard_map/add | solution.py:155
  305.1 1.1 copy-done.4
  306.2 1.1 copy-done.5
  307.3 3.5 divide_multiply_fusion
  310.8 4.1 %fusion = f32[455,4,4]{2,1,0:T(4,128)S(1)} fusion(f32[455,12,12]{2,1,0:T(8,128)} %get-tuple-element.54, f32[455,12,12]{2,1,0:T(8,128)S(1)} %get-tuple-element.47, f32[455,12,12]{2,1,0:T(8,128)S(1)} %get-tuple-element.53, f32[455,12,12]{2,1,0:T(8,128)S(1)} %add.320, f32[455,12,12]{2,1,0:T(8,128)S(1)} %get-tuple-element.48, f32[4,4]{1,0:T(4,128)S(1)} %copy-done.22, ...), kind=kLoop, calls=%fused_computation.22 | loop fusion | flops 72800 | bytes 174800 | tf_op jit(solution)/shard_map/add | solution.py:166
  315.1 3.5 gather_fusion.1
  318.7 4.3 %broadcast_select_fusion = f32[960,4,4]{2,1,0:T(4,128)} fusion(f32[960,4,4]{2,1,0:T(4,128)S(1)} %gather_fusion.1, pred[960]{0:T(1024)(128)(4,1)S(1)} %copy-done.23), kind=kLoop, calls=%fused_computation.20 | loop fusion | flops 15360 | bytes 123840 | tf_op jit(solution)/shard_map/jit(_take)/select_n | solution.py:183
  323.0 2.6 select_n.133
  325.6 1.9 select_reduce_fusion
  327.6 2.1 pad_maximum_fusion.3
  329.7 11.7 %all_to_all.17 = f32[32,1,483]{2,1,0:T(1,128)S(1)} all-to-all(f32[32,1,483]{2,1,0:T(1,128)S(1)} %copy.108), channel_id=1, replica_groups=mesh['space'=16,'chaos'=32] {'chaos'}, dimensions={0} | all-to-all | bytes 123648 | tf_op jit(solution)/shard_map/all_to_all | solution.py:192
  342.6 37.2 %psum.7 = f32[3]{0:T(128)S(1)} all-reduce(f32[3]{0:T(128)S(1)} %slice_reduce_fusion), channel_id=1, replica_groups=mesh['space'=16,'chaos'=32] {'space'}, use_global_device_ids=true, to_apply=%region_9.11 | all-reduce | flops 3 | bytes 24 | tf_op jit(solution)/shard_map/psum | solution.py:196
  (129 shorter events, 25.1 us)
Async XLA Ops:
  2.9 34.0 %collective-permute-start = (f32[43,4,128]{2,1,0:T(4,128)S(1)}, f32[43,4,128]{2,1,0:T(4,128)S(1)}, u32[]{:S(2)}, u32[]{:S(2)}) collective-permute-start(f32[43,4,128]{2,1,0:T(4,128)S(1)} %pad_maximum_fusion.2), channel_id=1, source_target_pairs={{0,32},{32,64},{64,96},{96,128},{128,160},{160,192},{192,224},{224... | collective-permute-start | bytes 264200 | tf_op jit(solution)/shard_map/ppermute | solution.py:95
  6.8 30.2 %collective-permute-start.1 = (f32[43,4,128]{2,1,0:T(4,128)S(1)}, f32[43,4,128]{2,1,0:T(4,128)S(1)}, u32[]{:S(2)}, u32[]{:S(2)}) collective-permute-start(f32[43,4,128]{2,1,0:T(4,128)S(1)} %pad_maximum_fusion.2), channel_id=1, source_target_pairs={{32,0},{64,32},{96,64},{128,96},{160,128},{192,160},{224,192},{256... | collective-permute-start | bytes 264200 | tf_op jit(solution)/shard_map/ppermute | solution.py:96
  11.3 0.6 copy-start.19
  40.6 1.7 copy-start.10
  45.2 17.8 %all-to-all-start = ((f32[32,1,4320]{2,1,0:T(1,128)}), f32[32,1,4320]{2,1,0:T(1,128)S(1)}, u32[]{:S(2)}, u32[]{:S(2)}) async-start(f32[32,1,4320]{2,1,0:T(1,128)} %reshape.541), calls=%async_computation | async-start | bytes 1114112 | tf_op jit(solution)/shard_map/all_to_all | solution.py:106
  54.9 8.6 %copy-start.17 = (f32[12,12]{1,0:T(8,128)}, f32[12,12]{1,0:T(8,128)S(1)}, u32[]{:S(2)}) copy-start(f32[12,12]{1,0:T(8,128)S(1)} %div.43) | copy-start | bytes 1732
  77.0 2.5 copy-start.6
  79.4 2.6 copy-start
  131.8 4.7 %copy-start.15 = (f32[12,455]{1,0:T(8,128)S(1)}, f32[12,455]{1,0:T(8,128)}, u32[]{:S(2)}) copy-start(f32[12,455]{1,0:T(8,128)} %constant.163) | copy-start | bytes 65524
  131.8 4.7 %copy-start.16 = (f32[12,455]{1,0:T(8,128)S(1)}, f32[12,455]{1,0:T(8,128)}, u32[]{:S(2)}) copy-start(f32[12,455]{1,0:T(8,128)} %constant.164) | copy-start | bytes 65524
  136.5 5.8 %copy-start.7 = (f32[455,144]{1,0:T(8,128)S(1)}, f32[455,144]{1,0:T(8,128)}, u32[]{:S(2)}) copy-start(f32[455,144]{1,0:T(8,128)} %copy-done.6) | copy-start | bytes 786244
  143.6 71.6 %copy-start.8 = (f32[455,144]{1,0:T(8,128)}, f32[455,144]{1,0:T(8,128)S(1)}, u32[]{:S(2)}) copy-start(f32[455,144]{1,0:T(8,128)S(1)} %get-tuple-element.44) | copy-start | bytes 786244
  145.8 2.6 copy-start.1
  219.4 2.6 copy-start.2
  281.6 6.7 %copy-start.13 = (f32[455,12,12]{0,2,1:T(8,128)S(1)}, f32[455,12,12]{0,2,1:T(8,128)}, u32[]{:S(2)}) copy-start(f32[455,12,12]{0,2,1:T(8,128)} %reduce_sum.83) | copy-start | bytes 786244
  287.3 3.8 slice-start.1
  287.3 7.3 %copy-start.14 = (f32[455,12,12]{0,2,1:T(8,128)S(1)}, f32[455,12,12]{0,2,1:T(8,128)}, u32[]{:S(2)}) copy-start(f32[455,12,12]{0,2,1:T(8,128)} %reduce_sum.81) | copy-start | bytes 786244
  291.0 6.3 %slice-start = ((f32[13,455,144]{2,1,0:T(8,128)}), f32[1,455,144]{2,1,0:T(8,128)S(1)}, s32[]{:S(2)}) async-start(f32[13,455,144]{2,1,0:T(8,128)} %copy-done), calls=%async_computation.2 | async-start | bytes 933888 | tf_op jit(solution)/shard_map/slice | solution.py:155
  294.6 10.1 %copy-start.18 = (f32[12,12]{1,0:T(8,128)S(1)}, f32[12,12]{1,0:T(8,128)}, u32[]{:S(2)}) copy-start(f32[12,12]{1,0:T(8,128)} %copy-done.17) | copy-start | bytes 1732
  294.6 10.1 %copy-start.20 = (pred[12,12]{1,0:T(8,128)(4,1)S(1)}, pred[12,12]{1,0:T(8,128)(4,1)}, u32[]{:S(2)}) copy-start(pred[12,12]{1,0:T(8,128)(4,1)} %copy-done.19) | copy-start | bytes 436
  300.8 4.2 %copy-start.3 = (f32[455,12,12]{2,1,0:T(8,128)S(1)}, f32[455,12,12]{2,1,0:T(8,128)}, u32[]{:S(2)}) copy-start(f32[455,12,12]{2,1,0:T(8,128)} %reshape.507) | copy-start | bytes 786244
  300.8 5.4 %copy-start.4 = (f32[455,12,12]{2,1,0:T(8,128)S(1)}, f32[455,12,12]{2,1,0:T(8,128)}, u32[]{:S(2)}) copy-start(f32[455,12,12]{2,1,0:T(8,128)} %copy.97) | copy-start | bytes 786244
  300.8 6.4 %copy-start.5 = (f32[455,12,12]{2,1,0:T(8,128)S(1)}, f32[455,12,12]{2,1,0:T(8,128)}, u32[]{:S(2)}) copy-start(f32[455,12,12]{2,1,0:T(8,128)} %reshape.509) | copy-start | bytes 786244
  307.3 3.5 copy-start.22
  307.3 3.5 copy-start.25
  310.8 4.3 %copy-start.21 = (s32[1024]{0:T(1024)S(1)}, s32[1024]{0:T(1024)}, u32[]{:S(2)}) copy-start(s32[1024]{0:T(1024)} %pad_clamp_fusion.2) | copy-start | bytes 12292
  310.8 7.8 %copy-start.23 = (pred[960]{0:T(1024)(128)(4,1)S(1)}, pred[960]{0:T(1024)(128)(4,1)}, u32[]{:S(2)}) copy-start(pred[960]{0:T(1024)(128)(4,1)} %compare_and_fusion) | copy-start | bytes 2884
  315.1 10.5 %copy-start.9 = (f32[455,144]{1,0:T(8,128)S(1)}, f32[455,144]{1,0:T(8,128)}, u32[]{:S(2)}) copy-start(f32[455,144]{1,0:T(8,128)} %copy-done.8) | copy-start | bytes 786244
  315.1 10.5 %copy-start.24 = (pred[144]{0:T(512)(128)(4,1)S(1)}, pred[144]{0:T(512)(128)(4,1)}, u32[]{:S(2)}) copy-start(pred[144]{0:T(512)(128)(4,1)} %and.113) | copy-start | bytes 436
  318.7 6.9 %copy-start.11 = (f32[455,144]{1,0:T(8,128)S(1)}, f32[455,144]{1,0:T(8,128)}, u32[]{:S(2)}) copy-start(f32[455,144]{1,0:T(8,128)} %copy.107) | copy-start | bytes 786244
  318.7 6.9 %copy-start.12 = (f32[455,144]{1,0:T(8,128)S(1)}, f32[455,144]{1,0:T(8,128)}, u32[]{:S(2)}) copy-start(f32[455,144]{1,0:T(8,128)} %get-tuple-element.42) | copy-start | bytes 786244
